TPU v7x, 32 devices: a whole 2x2x4 slice. The times are simulated.
32 devices in a mesh: grp: 2 (over x), blade: 8 (over z, y), dof: 2 (over core).
Axes of the slice: x: 2, y: 2, z: 4, core: 2. Of those that a mesh axis runs over, the one named last changes fastest.
Arguments:
- panel: bfloat16 [8192, 512], P(('grp', 'blade', 'dof')), parts along dimension 0, may hold values from -0.25 to 0.25
- stiffness: bfloat16 [96, 64, 128, 128], P(('grp', 'blade'), 'dof'), parts along dimension 0, may hold values from -0.5 to 0.5
- block_rows: int32 [96, 64], P(('grp', 'blade'), 'dof'), parts along dimension 0, may hold values from 0 to 31
- block_cols: int32 [96, 64], P(('grp', 'blade'), 'dof'), parts along dimension 0, may hold values from 0 to 31
Outputs:
- spectral: float32 [2, 96, 512, 512], P(None, ('grp', 'blade'), 'dof'), parts along dimension 1
There are 2 independent parts, one for each index of `grp`. A program takes and returns all parts, laid end to end along the dimension named above; each array names one. Nothing has to cross between parts.
Inputs may be any that keep to these rules, and one draw needn't show every extreme that they name: `block_rows`: row block index of each stiffness block; indices of one blade may repeat. `block_cols`: column block index of each stiffness block; indices of one blade may repeat.
All inputs are finite; a program needn't handle non-finite values.
Results may differ from a plain program's by a relative error of at most 0.0029.
Values may be sent and summed in bfloat16 or wider, within the bound.
No kernel may reach another device: no remote copies, remote signals or barrier semaphores. Data moves between devices by JAX's collectives and lax.ppermute only.
A program may use at most 128 MiB of HBM per device.

v0:
```python
import math
import jax
import jax.numpy as jnp
from jax import lax
from jax.sharding import PartitionSpec as P


def body(panel, stiffness, block_rows, block_cols):
    block_size = stiffness.shape[-1]
    modes = panel.shape[-1]
    whole = lax.all_gather(panel, ("blade", "dof"), axis=0, tiled=True)
    blocks = whole.reshape(-1, block_size, modes)

    def one_blade(items):
        mats, rows, cols = items
        chosen = jnp.take(blocks, cols, axis=0)
        image = jnp.einsum("nij,njm->nim", mats, chosen, preferred_element_type=jnp.float32)
        image = image.astype(jnp.bfloat16)
        left = jnp.take(blocks, rows, axis=0).reshape(-1, modes)
        return lax.dot_general(
            left,
            image.reshape(-1, modes),
            (((0,), (0,)), ((), ())),
            preferred_element_type=jnp.float32,
        )

    partial_proj = lax.map(one_blade, (stiffness, block_rows, block_cols))
    blade_count = stiffness.shape[0] * lax.axis_size("blade")
    index = jnp.arange(blade_count, dtype=jnp.int32)
    angle = (index[:, None] * index[None, :] % blade_count).astype(jnp.float32) * (
        2.0 * math.pi / blade_count
    )
    cosine = jnp.cos(angle)
    sine = jnp.sin(angle)
    stacked = lax.all_to_all(partial_proj, "blade", split_axis=1, concat_axis=0, tiled=True)
    real_part = jnp.einsum("hb,brc->hrc", cosine, stacked, precision=lax.Precision.HIGHEST)
    imag_part = -jnp.einsum("hb,brc->hrc", sine, stacked, precision=lax.Precision.HIGHEST)
    joined = jnp.stack([real_part, imag_part])
    full_spec = lax.all_to_all(joined, "blade", split_axis=1, concat_axis=2, tiled=True)
    result = lax.psum_scatter(full_spec, "dof", scatter_dimension=2, tiled=True)
    return result


def solution(mesh):
    placed = (
        P(("grp", "blade", "dof"), None),
        P(("grp", "blade"), "dof", None, None),
        P(("grp", "blade"), "dof"),
        P(("grp", "blade"), "dof"),
    )
    return jax.shard_map(
        body,
        mesh=mesh,
        in_specs=placed,
        out_specs=P(None, ("grp", "blade"), "dof", None),
        check_vma=False,
    )
```

profile of v0, /device:TPU:0, one launch (start us, length us, event | category | flops | bytes accessed | tf_op | source)
XLA Modules:
  0.0 863.4 jit_solution(7075036304253567163)
XLA Ops:
  7.3 55.5 %all-gather.2.cloned.1.call-done = bf16[4096,512]{1,0:T(8,128)(2,1)} async-done(((bf16[256,512]{1,0:T(8,128)(2,1)}), bf16[4096,512]{1,0:T(8,128)(2,1)}) %all-gather.2.cloned.1.call-update) | async-done | bytes 4194320 | tf_op jit(solution)/shard_map/all_gather | solution.py:11
  62.8 244.8 %while.10 = (s32[]{:T(128)}, f32[6,512,512]{2,0,1:T(8,128)}, s32[6,32]{1,0:T(8,128)}, bf16[32,128,512]{2,1,0:T(8,128)(2,1)}, bf16[6,32,128,128]{3,2,1,0:T(8,128)...) while((s32[]{:T(128)}, f32[6,512,512]{2,0,1:T(8,128)}, s32[6,32]{1,0:T(8,128)}, ...), condition=%wide.region_1.3_spmd, body=%wide.region_0.2_spmd.sunk | while | flops 2690648576 | bytes 31466728 | solution.py:27
  68.5 5.0 gather_fusion
  73.5 7.2 fusion.71
  81.8 21.8 %dynamic_update_slice.5 = f32[6,512,512]{2,0,1:T(8,128)} dynamic-update-slice(f32[6,512,512]{2,0,1:T(8,128)} %get-tuple-element.111, f32[1,512,512]{2,0,1:T(1,128)S(1)} %copy.41, s32[]{:T(128)S(6)} %copy.45, s32[]{:T(128)} %constant.36.clone.1..sunk, s32[]{:T(128)} %constant.36.clone.1..sunk) | dynamic-update-slice | bytes 2097156 | tf_op jit(solution)/shard_map/while/body/jit(dynamic_update_index_in_dim)/dynamic_update_slice | solution.py:27
  109.3 5.0 gather_fusion
  114.3 7.2 fusion.71
  122.6 21.8 %dynamic_update_slice.5 = f32[6,512,512]{2,0,1:T(8,128)} dynamic-update-slice(f32[6,512,512]{2,0,1:T(8,128)} %get-tuple-element.111, f32[1,512,512]{2,0,1:T(1,128)S(1)} %copy.41, s32[]{:T(128)S(6)} %copy.45, s32[]{:T(128)} %constant.36.clone.1..sunk, s32[]{:T(128)} %constant.36.clone.1..sunk) | dynamic-update-slice | bytes 2097156 | tf_op jit(solution)/shard_map/while/body/jit(dynamic_update_index_in_dim)/dynamic_update_slice | solution.py:27
  155.1 7.2 fusion.71
  163.4 21.8 %dynamic_update_slice.5 = f32[6,512,512]{2,0,1:T(8,128)} dynamic-update-slice(f32[6,512,512]{2,0,1:T(8,128)} %get-tuple-element.111, f32[1,512,512]{2,0,1:T(1,128)S(1)} %copy.41, s32[]{:T(128)S(6)} %copy.45, s32[]{:T(128)} %constant.36.clone.1..sunk, s32[]{:T(128)} %constant.36.clone.1..sunk) | dynamic-update-slice | bytes 2097156 | tf_op jit(solution)/shard_map/while/body/jit(dynamic_update_index_in_dim)/dynamic_update_slice | solution.py:27
  195.9 7.2 fusion.71
  204.2 21.8 %dynamic_update_slice.5 = f32[6,512,512]{2,0,1:T(8,128)} dynamic-update-slice(f32[6,512,512]{2,0,1:T(8,128)} %get-tuple-element.111, f32[1,512,512]{2,0,1:T(1,128)S(1)} %copy.41, s32[]{:T(128)S(6)} %copy.45, s32[]{:T(128)} %constant.36.clone.1..sunk, s32[]{:T(128)} %constant.36.clone.1..sunk) | dynamic-update-slice | bytes 2097156 | tf_op jit(solution)/shard_map/while/body/jit(dynamic_update_index_in_dim)/dynamic_update_slice | solution.py:27
  236.7 7.2 fusion.71
  245.0 21.8 %dynamic_update_slice.5 = f32[6,512,512]{2,0,1:T(8,128)} dynamic-update-slice(f32[6,512,512]{2,0,1:T(8,128)} %get-tuple-element.111, f32[1,512,512]{2,0,1:T(1,128)S(1)} %copy.41, s32[]{:T(128)S(6)} %copy.45, s32[]{:T(128)} %constant.36.clone.1..sunk, s32[]{:T(128)} %constant.36.clone.1..sunk) | dynamic-update-slice | bytes 2097156 | tf_op jit(solution)/shard_map/while/body/jit(dynamic_update_index_in_dim)/dynamic_update_slice | solution.py:27
  277.5 7.2 fusion.71
  285.8 21.8 %dynamic_update_slice.5 = f32[6,512,512]{2,0,1:T(8,128)} dynamic-update-slice(f32[6,512,512]{2,0,1:T(8,128)} %get-tuple-element.111, f32[1,512,512]{2,0,1:T(1,128)S(1)} %copy.41, s32[]{:T(128)S(6)} %copy.45, s32[]{:T(128)} %constant.36.clone.1..sunk, s32[]{:T(128)} %constant.36.clone.1..sunk) | dynamic-update-slice | bytes 2097156 | tf_op jit(solution)/shard_map/while/body/jit(dynamic_update_index_in_dim)/dynamic_update_slice | solution.py:27
  307.6 187.5 %all_to_all.36 = f32[6,512,512]{2,0,1:T(8,128)S(1)} all-to-all(f32[6,512,512]{2,0,1:T(8,128)} %get-tuple-element.38), channel_id=1, replica_groups=mesh['grp'=2,'blade'=8,'dof'=2] {'blade'}, dimensions={1} | all-to-all | bytes 12582912 | tf_op jit(solution)/shard_map/all_to_all | solution.py:35
  498.6 9.7 %negate_bitcast_fusion = f32[1,48,64,512]{3,1,2,0:T(8,128)S(1)} fusion(f32[48,64,512]{2,1,0:T(8,128)S(1)} %bitcast.41), kind=kOutput, calls=%fused_computation.26 | convolution fusion | flops 907563264 | bytes 12582912 | tf_op jit(solution)/shard_map/hb,brc->hrc/dot_general | solution.py:37
  508.3 10.2 %fusion.34 = f32[1,48,64,512]{3,1,2,0:T(8,128)} fusion(f32[48,64,512]{2,1,0:T(8,128)S(1)} %bitcast.42), kind=kOutput, calls=%fused_computation.31 | convolution fusion | flops 905990400 | bytes 12582912 | tf_op jit(solution)/shard_map/hb,brc->hrc/dot_general | solution.py:36
  518.5 9.5 %pad_maximum_fusion = f32[2,48,64,512]{3,1,2,0:T(8,128)} fusion(f32[1,48,64,512]{3,1,2,0:T(8,128)S(1)} %negate_bitcast_fusion, f32[1,48,64,512]{3,1,2,0:T(8,128)} %fusion.34), kind=kLoop, calls=%fused_computation.25 | loop fusion | flops 3145728 | bytes 25165824 | tf_op jit(solution)/shard_map/stack | solution.py:38
  528.0 16.4 %copy.24 = f32[2,48,64,512]{3,2,0,1:T(8,128)} copy(f32[2,48,64,512]{3,1,2,0:T(8,128)} %pad_maximum_fusion) | data formatting | bytes 25165824 | tf_op jit(solution)/shard_map/stack | solution.py:38
  544.4 279.6 %all_to_all.37 = f32[2,48,64,512]{3,2,0,1:T(8,128)} all-to-all(f32[2,48,64,512]{3,2,0,1:T(8,128)} %copy.24), channel_id=1, replica_groups=mesh['grp'=2,'blade'=8,'dof'=2] {'blade'}, dimensions={1} | all-to-all | bytes 25165824 | tf_op jit(solution)/shard_map/all_to_all | solution.py:39
  823.9 12.0 %copy.26 = f32[2,6,8,64,512]{4,3,2,1,0:T(8,128)} copy(f32[2,6,8,64,512]{4,3,0,1,2:T(8,128)} %bitcast.44) | data formatting | bytes 25165824 | tf_op jit(solution)/shard_map/all_to_all | solution.py:39
  835.9 20.6 %reduce-scatter.2.cloned.1.call-done = f32[2,6,256,512]{3,2,1,0:T(8,128)} async-done(((f32[2,6,512,512]{3,2,1,0:T(8,128)}), f32[2,6,256,512]{3,2,1,0:T(8,128)}) %reduce-scatter.2.cloned.1.call-update) | async-done | bytes 6291472 | tf_op jit(solution)/shard_map/reduce_scatter | solution.py:40
  (40 shorter events, 64.9 us)
Async XLA Ops:
  6.5 56.3 %all-gather.2.cloned.1.call-start = ((), (), s32[]{:S(2)}) async-start(), calls=%async_computation.3 | async-start | bytes 4456448 | tf_op jit(solution)/shard_map/all_gather | solution.py:11
  7.3 849.3 %reduce-scatter.2.cloned.1.call-start = ((), (), s32[]{:S(2)}) async-start(), calls=%async_computation.4 | async-start | bytes 18874368 | tf_op jit(solution)/shard_map/reduce_scatter | solution.py:40
Sparse Core Ops, SparseCore 0:
  9.5 53.2 all-gather.1
  836.0 20.4 reduce-scatter.1
where the time goes:
time: 868 us; the launch traced here: 863 us
  blocking collectives  467 us (54%)
  local copies, waits for them, and re-layouts  229 us (26%)
  waiting for transfers between devices  76.9 us (9%)
  matrix products  63.3 us (7%)
  other arithmetic  13.8 us (2%)
  between operations  13.4 us (2%)
    all_to_all x1, blocking collectives, body(): lax.all_to_all(joined, 'blade', split_axis=1, concat_axis=2, tiled=True)  280 us
    all_to_all x1, blocking collectives, body(): lax.all_to_all(partial_proj, 'blade', split_axis=1, concat_axis=0, tiled=...  187 us
    dynamic_update_slice x12, local copies, waits for them, and re-layouts, body(): partial_proj = lax.map(one_blade, (stiffness, block_rows, block_cols))  137 us
    all_gather x1, waiting for transfers between devices, body(): whole = lax.all_gather(panel, ('blade', 'dof'), axis=0, tiled=True)  55.5 us
    dot_general x6, matrix products, one_blade(): lax.dot_general(left, image.reshape(-1, modes), (((0,), (0,)), ((), ())),...  43.5 us
    gather x6, local copies, waits for them, and re-layouts, one_blade(): chosen = jnp.take(blocks, cols, axis=0)  30.1 us
    gather x6, local copies, waits for them, and re-layouts, one_blade(): left = jnp.take(blocks, rows, axis=0).reshape(-1, modes)  29.7 us
    reduce_scatter x1, waiting for transfers between devices, body(): result = lax.psum_scatter(full_spec, 'dof', scatter_dimension=2, tiled=True)  20.6 us
  transfers between devices with their start and end apart: 2, of which 2 were waited for; matrix products, arithmetic and copies ran while one was open for 0% of the time, Pallas kernels for 0%

commit v1 on v0

--- a/solution.py
+++ b/solution.py
@@ -1,14 +1,47 @@
+import functools
 import math
 import jax
 import jax.numpy as jnp
 from jax import lax
 from jax.sharding import PartitionSpec as P
+from jax.lax import axis_index, axis_size, ppermute
+
+
+def balance_view(mine_x, array_dim):
+    met_up, new, part_next = (
+        axis_size(("blade", "dof")),
+        axis_index(("blade", "dof")),
+        mine_x.shape[array_dim],
+    )
+    entries = list(map(lambda m: (m, (m + 1) % met_up), range(met_up)))
+    parts_seen = list(map(lambda m: (m, (m - 1) % met_up), range(met_up)))
+    reached = jnp.zeros(
+        (*mine_x.shape[:array_dim], met_up * part_next, *mine_x.shape[array_dim + 1 :]),
+        mine_x.dtype,
+    )
+    reached = lax.dynamic_update_slice_in_dim(reached, mine_x, new * part_next, axis=array_dim)
+    small = item_now = mine_x
+    carry = met_up // 2
+    for to_i in range(1, carry + 1):
+        small = ppermute(small, ("blade", "dof"), entries)
+        reached = lax.dynamic_update_slice_in_dim(
+            reached, small, (new - to_i) % met_up * part_next, axis=array_dim
+        )
+        if to_i < met_up - carry:
+            item_now = ppermute(item_now, ("blade", "dof"), parts_seen)
+            reached = lax.dynamic_update_slice_in_dim(
+                reached, item_now, (new + to_i) % met_up * part_next, axis=array_dim
+            )
+    return reached
+
+
+switch_the_cells = functools.partial(balance_view, array_dim=0)
 
 
 def body(panel, stiffness, block_rows, block_cols):
     block_size = stiffness.shape[-1]
     modes = panel.shape[-1]
-    whole = lax.all_gather(panel, ("blade", "dof"), axis=0, tiled=True)
+    whole = switch_the_cells(panel)
     blocks = whole.reshape(-1, block_size, modes)
 
     def one_blade(items):

time: 868 us -> 895 us (1.031)
  starting transfers between devices: 0.04 us -> 32.9 us
  waiting for transfers between devices: 76.9 us -> 45.3 us
  local copies, waits for them, and re-layouts: 229 us -> 242 us
  matrix products: 63.3 us -> 74.2 us
    all_gather x1 -> x0, waiting for transfers between devices: 55.5 us -> none  [body(): whole = lax.all_gather(panel, ('blade', 'dof'), axis=0, tiled=True)]
    ppermute x0 -> x15, starting transfers between devices: none -> 32.9 us  [the longest x7 32.4 us: balance_view(): item_now = ppermute(item_now, ('blade', 'dof'), parts_seen)]
    ppermute x0 -> x15, waiting for transfers between devices: none -> 24.3 us  [the longest x8 17.5 us: balance_view(): small = ppermute(small, ('blade', 'dof'), entries)]
    dynamic_update_slice x0 -> x16, local copies, waits for them, and re-layouts: none -> 11.5 us  [the longest x8 5.75 us: balance_view(): lax.dynamic_update_slice_in_dim(reached, small, (new - to_i) % met_up * p...]
    dot_general x1, matrix products: 9.7 us -> 20.6 us  [body(): jnp.einsum('hb,brc->hrc', sine, stacked, precision=lax.Precision.HIGHEST)]
  transfers between devices with their start and end apart: 2 -> 16, of which waited for: 2 -> 9; matrix products, arithmetic and copies ran while one was open for 0% -> 1% of each run, Pallas kernels for 0% -> 0%
where the time goes in v1:
time: 895 us; the launch traced here: 884 us
  blocking collectives  463 us (52%)
  local copies, waits for them, and re-layouts  242 us (27%)
  matrix products  74.2 us (8%)
  waiting for transfers between devices  45.3 us (5%)
  starting transfers between devices  32.9 us (4%)
  other arithmetic  13.8 us (2%)
  between operations  13.4 us (1%)
    all_to_all x1, blocking collectives, body(): lax.all_to_all(joined, 'blade', split_axis=1, concat_axis=2, tiled=True)  278 us
    all_to_all x1, blocking collectives, body(): lax.all_to_all(partial_proj, 'blade', split_axis=1, concat_axis=0, tiled=...  185 us
    dynamic_update_slice x12, local copies, waits for them, and re-layouts, body(): partial_proj = lax.map(one_blade, (stiffness, block_rows, block_cols))  137 us
    dot_general x6, matrix products, one_blade(): lax.dot_general(left, image.reshape(-1, modes), (((0,), (0,)), ((), ())),...  43.5 us
    ppermute x7, starting transfers between devices, balance_view(): item_now = ppermute(item_now, ('blade', 'dof'), parts_seen)  32.4 us
    gather x6, local copies, waits for them, and re-layouts, one_blade(): chosen = jnp.take(blocks, cols, axis=0)  29.8 us
    gather x6, local copies, waits for them, and re-layouts, one_blade(): left = jnp.take(blocks, rows, axis=0).reshape(-1, modes)  29.6 us
    reduce_scatter x1, waiting for transfers between devices, body(): result = lax.psum_scatter(full_spec, 'dof', scatter_dimension=2, tiled=True)  20.9 us
  transfers between devices with their start and end apart: 16, of which 9 were waited for; matrix products, arithmetic and copies ran while one was open for 1% of the time, Pallas kernels for 0%

profile of v1, /device:TPU:0, one launch (start us, length us, event | category | flops | bytes accessed | tf_op | source)
XLA Modules:
  0.0 884.4 jit_solution(2536369516847637638)
XLA Ops:
  7.0 5.0 collective-permute-start.1
  77.5 244.1 %while.10 = (s32[]{:T(128)}, f32[6,512,512]{2,0,1:T(8,128)}, s32[6,32]{1,0:T(8,128)}, bf16[32,128,512]{2,1,0:T(8,128)(2,1)}, bf16[6,32,128,128]{3,2,1,0:T(8,128)...) while((s32[]{:T(128)}, f32[6,512,512]{2,0,1:T(8,128)}, s32[6,32]{1,0:T(8,128)}, ...), condition=%wide.region_1.3_spmd, body=%wide.region_0.2_spmd.sunk | while | flops 2690648576 | bytes 31466728 | solution.py:60
  83.2 5.0 gather_fusion
  88.2 7.2 fusion.71
  96.5 21.7 %dynamic_update_slice.85 = f32[6,512,512]{2,0,1:T(8,128)} dynamic-update-slice(f32[6,512,512]{2,0,1:T(8,128)} %get-tuple-element.111, f32[1,512,512]{2,0,1:T(1,128)S(1)} %copy.41, s32[]{:T(128)S(6)} %copy.61, s32[]{:T(128)} %constant.127.clone.1..sunk, s32[]{:T(128)} %constant.127.clone.1..sunk) | dynamic-update-slice | bytes 2097156 | tf_op jit(solution)/shard_map/while/body/jit(dynamic_update_index_in_dim)/dynamic_update_slice | solution.py:60
  123.9 5.0 gather_fusion
  128.9 7.2 fusion.71
  137.2 21.7 %dynamic_update_slice.85 = f32[6,512,512]{2,0,1:T(8,128)} dynamic-update-slice(f32[6,512,512]{2,0,1:T(8,128)} %get-tuple-element.111, f32[1,512,512]{2,0,1:T(1,128)S(1)} %copy.41, s32[]{:T(128)S(6)} %copy.61, s32[]{:T(128)} %constant.127.clone.1..sunk, s32[]{:T(128)} %constant.127.clone.1..sunk) | dynamic-update-slice | bytes 2097156 | tf_op jit(solution)/shard_map/while/body/jit(dynamic_update_index_in_dim)/dynamic_update_slice | solution.py:60
  169.5 7.2 fusion.71
  177.9 21.7 %dynamic_update_slice.85 = f32[6,512,512]{2,0,1:T(8,128)} dynamic-update-slice(f32[6,512,512]{2,0,1:T(8,128)} %get-tuple-element.111, f32[1,512,512]{2,0,1:T(1,128)S(1)} %copy.41, s32[]{:T(128)S(6)} %copy.61, s32[]{:T(128)} %constant.127.clone.1..sunk, s32[]{:T(128)} %constant.127.clone.1..sunk) | dynamic-update-slice | bytes 2097156 | tf_op jit(solution)/shard_map/while/body/jit(dynamic_update_index_in_dim)/dynamic_update_slice | solution.py:60
  210.2 7.2 fusion.71
  218.5 21.7 %dynamic_update_slice.85 = f32[6,512,512]{2,0,1:T(8,128)} dynamic-update-slice(f32[6,512,512]{2,0,1:T(8,128)} %get-tuple-element.111, f32[1,512,512]{2,0,1:T(1,128)S(1)} %copy.41, s32[]{:T(128)S(6)} %copy.61, s32[]{:T(128)} %constant.127.clone.1..sunk, s32[]{:T(128)} %constant.127.clone.1..sunk) | dynamic-update-slice | bytes 2097156 | tf_op jit(solution)/shard_map/while/body/jit(dynamic_update_index_in_dim)/dynamic_update_slice | solution.py:60
  250.9 7.2 fusion.71
  259.2 21.7 %dynamic_update_slice.85 = f32[6,512,512]{2,0,1:T(8,128)} dynamic-update-slice(f32[6,512,512]{2,0,1:T(8,128)} %get-tuple-element.111, f32[1,512,512]{2,0,1:T(1,128)S(1)} %copy.41, s32[]{:T(128)S(6)} %copy.61, s32[]{:T(128)} %constant.127.clone.1..sunk, s32[]{:T(128)} %constant.127.clone.1..sunk) | dynamic-update-slice | bytes 2097156 | tf_op jit(solution)/shard_map/while/body/jit(dynamic_update_index_in_dim)/dynamic_update_slice | solution.py:60
  291.6 7.2 fusion.71
  299.9 21.7 %dynamic_update_slice.85 = f32[6,512,512]{2,0,1:T(8,128)} dynamic-update-slice(f32[6,512,512]{2,0,1:T(8,128)} %get-tuple-element.111, f32[1,512,512]{2,0,1:T(1,128)S(1)} %copy.41, s32[]{:T(128)S(6)} %copy.61, s32[]{:T(128)} %constant.127.clone.1..sunk, s32[]{:T(128)} %constant.127.clone.1..sunk) | dynamic-update-slice | bytes 2097156 | tf_op jit(solution)/shard_map/while/body/jit(dynamic_update_index_in_dim)/dynamic_update_slice | solution.py:60
  321.6 184.9 %all_to_all.36 = f32[6,512,512]{2,0,1:T(8,128)S(1)} all-to-all(f32[6,512,512]{2,0,1:T(8,128)} %get-tuple-element.38), channel_id=1, replica_groups=mesh['grp'=2,'blade'=8,'dof'=2] {'blade'}, dimensions={1} | all-to-all | bytes 12582912 | tf_op jit(solution)/shard_map/all_to_all | solution.py:68
  510.0 20.6 %negate_bitcast_fusion = f32[1,48,64,512]{3,1,2,0:T(8,128)S(1)} fusion(f32[48,64,512]{2,1,0:T(8,128)S(1)} %bitcast.40), kind=kOutput, calls=%fused_computation.26 | convolution fusion | flops 907563264 | bytes 12582912 | tf_op jit(solution)/shard_map/hb,brc->hrc/dot_general | solution.py:70
  530.6 10.2 %fusion.34 = f32[1,48,64,512]{3,1,2,0:T(8,128)} fusion(f32[48,64,512]{2,1,0:T(8,128)S(1)} %bitcast.41), kind=kOutput, calls=%fused_computation.31 | convolution fusion | flops 905990400 | bytes 12582912 | tf_op jit(solution)/shard_map/hb,brc->hrc/dot_general | solution.py:69
  540.8 9.5 %pad_maximum_fusion = f32[2,48,64,512]{3,1,2,0:T(8,128)} fusion(f32[1,48,64,512]{3,1,2,0:T(8,128)S(1)} %negate_bitcast_fusion, f32[1,48,64,512]{3,1,2,0:T(8,128)} %fusion.34), kind=kLoop, calls=%fused_computation.25 | loop fusion | flops 3145728 | bytes 25165824 | tf_op jit(solution)/shard_map/stack | solution.py:71
  550.3 16.4 %copy.24 = f32[2,48,64,512]{3,2,0,1:T(8,128)} copy(f32[2,48,64,512]{3,1,2,0:T(8,128)} %pad_maximum_fusion) | data formatting | bytes 25165824 | tf_op jit(solution)/shard_map/stack | solution.py:71
  566.7 278.0 %all_to_all.37 = f32[2,48,64,512]{3,2,0,1:T(8,128)} all-to-all(f32[2,48,64,512]{3,2,0,1:T(8,128)} %copy.24), channel_id=1, replica_groups=mesh['grp'=2,'blade'=8,'dof'=2] {'blade'}, dimensions={1} | all-to-all | bytes 25165824 | tf_op jit(solution)/shard_map/all_to_all | solution.py:72
  844.6 12.0 %copy.26 = f32[2,6,8,64,512]{4,3,2,1,0:T(8,128)} copy(f32[2,6,8,64,512]{4,3,0,1,2:T(8,128)} %bitcast.43) | data formatting | bytes 25165824 | tf_op jit(solution)/shard_map/all_to_all | solution.py:72
  856.6 20.9 %reduce-scatter.2.cloned.1.call-done = f32[2,6,256,512]{3,2,1,0:T(8,128)} async-done(((f32[2,6,512,512]{3,2,1,0:T(8,128)}), f32[2,6,256,512]{3,2,1,0:T(8,128)}) %reduce-scatter.2.cloned.1.call-update) | async-done | bytes 6291472 | tf_op jit(solution)/shard_map/reduce_scatter | solution.py:73
  (86 shorter events, 129.8 us)
Async XLA Ops:
  6.5 29.4 %copy-start = (bf16[256,512]{1,0:T(8,128)(2,1)S(1)}, bf16[256,512]{1,0:T(8,128)(2,1)}, u32[]{:S(2)}) copy-start(bf16[256,512]{1,0:T(8,128)(2,1)} %param.8) | copy-start | bytes 786436
  6.5 871.0 %reduce-scatter.2.cloned.1.call-start = ((), (), s32[]{:S(2)}) async-start(), calls=%async_computation.3 | async-start | bytes 18874368 | tf_op jit(solution)/shard_map/reduce_scatter | solution.py:73
  6.5 9.9 %collective-permute-start = (bf16[256,512]{1,0:T(8,128)(2,1)}, bf16[256,512]{1,0:T(8,128)(2,1)S(1)}, u32[]{:S(2)}, u32[]{:S(2)}) collective-permute-start(bf16[256,512]{1,0:T(8,128)(2,1)} %param.8), channel_id=1, source_target_pairs={{0,1},{1,2},{2,3},{3,4},{4,5},{5,6},{6,7},{7,8},{8,9},{9,10},{10,1... | collective-permute-start | bytes 786440 | tf_op jit(solution)/shard_map/ppermute | solution.py:26
  7.0 9.4 %collective-permute-start.1 = (bf16[256,512]{1,0:T(8,128)(2,1)}, bf16[256,512]{1,0:T(8,128)(2,1)S(1)}, u32[]{:S(2)}, u32[]{:S(2)}) collective-permute-start(bf16[256,512]{1,0:T(8,128)(2,1)} %param.8), channel_id=1, source_target_pairs={{0,15},{1,0},{2,1},{3,2},{4,3},{5,4},{6,5},{7,6},{8,7},{9,8},{10,9... | collective-permute-start | bytes 786440 | tf_op jit(solution)/shard_map/ppermute | solution.py:31
  16.4 8.6 collective-permute-start.2
  16.4 8.6 collective-permute-start.3
  25.0 8.6 collective-permute-start.4
  25.0 12.3 %collective-permute-start.5 = (bf16[256,512]{1,0:T(8,128)(2,1)S(1)}, bf16[256,512]{1,0:T(8,128)(2,1)S(1)}, u32[]{:S(2)}, u32[]{:S(2)}) collective-permute-start(bf16[256,512]{1,0:T(8,128)(2,1)S(1)} %collective-permute-done.3), channel_id=1, source_target_pairs={{0,15},{1,0},{2,1},{3,2},{4,3},{5,4},{6,5},{7,6},{8,7},{9,8},{10,9... | collective-permute-start | bytes 786440 | tf_op jit(solution)/shard_map/ppermute | solution.py:31
  33.6 8.9 %collective-permute-start.6 = (bf16[256,512]{1,0:T(8,128)(2,1)S(1)}, bf16[256,512]{1,0:T(8,128)(2,1)S(1)}, u32[]{:S(2)}, u32[]{:S(2)}) collective-permute-start(bf16[256,512]{1,0:T(8,128)(2,1)S(1)} %collective-permute-done.4), channel_id=1, source_target_pairs={{0,1},{1,2},{2,3},{3,4},{4,5},{5,6},{6,7},{7,8},{8,9},{9,10},{10,1... | collective-permute-start | bytes 786440 | tf_op jit(solution)/shard_map/ppermute | solution.py:26
  37.4 8.3 collective-permute-start.7
  42.5 8.6 collective-permute-start.8
  45.7 8.6 collective-permute-start.9
  51.1 8.6 collective-permute-start.10
  54.3 8.6 collective-permute-start.11
  59.7 8.6 collective-permute-start.12
  62.9 8.6 collective-permute-start.13
  68.3 8.5 collective-permute-start.14
Sparse Core Ops, SparseCore 0:
  856.7 20.7 reduce-scatter.1
